TPU v7x, 256 devices: a whole 4x4x8 slice. The times are simulated.
256 devices in a mesh: leaf: 4 (over x), row: 4 (over y), col: 16 (over z, core).
Axes of the slice: x: 4, y: 4, z: 8, core: 2. Of those that a mesh axis runs over, the one named last changes fastest.
Arguments:
- local_inv: float32 [4, 4, 256, 128, 128], P('leaf', 'row', 'col'), may hold values from -2 to 2, as said below
- local_off: float32 [4, 4, 256, 2, 128, 128], P('leaf', 'row', 'col'), may hold values from -0.09375 to 0.09375
- local_dep: int32 [4, 4, 256, 2], P('leaf', 'row', 'col'), may hold values from 0 to 7
- local_rhs: float32 [4, 4, 256, 64, 128], P('leaf', 'row', 'col'), may hold values from -6 to 6
- top_inv: float32 [8, 4, 16, 128, 128], P(None, 'row', 'col'), may hold values from -2 to 2, as said below
- top_off: float32 [7, 4, 16, 4, 128, 128], P(None, 'row', 'col'), may hold values from -0.125 to 0.125
- top_dep: int32 [7, 4, 16, 4], P(None, 'row', 'col'), may hold values from 0 to 19
- top_rhs: float32 [8, 4, 16, 64, 128], P(None, 'row', 'col'), may hold values from -6 to 6
Outputs:
- local_sol: float32 [4, 4, 256, 64, 128], P('leaf', 'row', 'col')
- top_sol: float32 [8, 4, 16, 64, 128], P(None, 'row', 'col')
Inputs may be any that keep to these rules, and one draw needn't show every extreme that they name: `local_inv`: lower-triangular inverse diagonal blocks of a Cholesky factor: entry [t, s] is zero for s > t. `top_inv`: lower-triangular inverse diagonal blocks of a Cholesky factor: entry [t, s] is zero for s > t. `local_dep`: levels of ancestors owned by the supernode's own grid cell. `top_dep`: a value v < 16 names the supernode one level lower in cell (r, v); a value v >= 16 the one in cell (v - 16, c).
All inputs are finite; a program needn't handle non-finite values.
Results may differ from a plain program's by a relative error of at most 0.0001.
Values sent between devices are 32-bit elements; how exact they have to be, the bound alone decides.
No kernel may reach another device: no remote copies, remote signals or barrier semaphores. Data moves between devices by JAX's collectives and lax.ppermute only.
A program may use at most 64 MiB of HBM per device.

v0:
```python
import jax
import jax.numpy as jnp
from jax import lax
from jax.sharding import PartitionSpec as P

highest = lax.Precision.HIGHEST


def apply_inverse(inverse, block):
    return jnp.einsum("rs,ts->rt", block, inverse, precision=highest)


def apply_transpose(inverse, block):
    return jnp.einsum("rs,st->rt", block, inverse, precision=highest)


def shifted(value, axis, k):
    n = lax.axis_size(axis)
    return lax.ppermute(value, axis, [(i, (i + k) % n) for i in range(n)])


def select_sum(mask, stacked):
    mask = mask.reshape(mask.shape + (1,) * (stacked.ndim - 1))
    return jnp.sum(jnp.where(mask, stacked[None], 0.0), axis=1)


def spread_sum(mask, pieces):
    return jnp.sum(jnp.where(mask[:, :, None, None], pieces[:, None], 0.0), axis=0)


def gather_sources(block, col_pick, row_pick):
    by_col = lax.all_gather(block[None], "col", axis=0, tiled=True)
    n_row = lax.axis_size("row")
    by_shift = jnp.stack([block] + [shifted(block, "row", k) for k in range(1, n_row)])
    return select_sum(col_pick, by_col) + select_sum(row_pick, by_shift)


def push_back(pieces, col_pick, row_push):
    n_row = lax.axis_size("row")
    slots = spread_sum(col_pick, pieces)
    incoming = lax.all_to_all(slots, "col", 0, 0, tiled=True).sum(0)
    parts = spread_sum(row_push, pieces)
    incoming = incoming + parts[0]
    for k in range(1, n_row):
        incoming = incoming + shifted(parts[k], "row", k)
    return incoming


def solve_top(top_inverse, top_blocks, top_links, top_right, updates):
    levels = top_inverse.shape[0]
    width_cols = lax.axis_size("col")
    n_row = lax.axis_size("row")
    me_row = lax.axis_index("row")
    is_col = top_links < width_cols
    col_pick = top_links[..., None] == jnp.arange(width_cols, dtype=jnp.int32)
    pull = jnp.mod(me_row - (top_links - width_cols), n_row)
    push = jnp.mod(top_links - width_cols - me_row, n_row)
    shifts = jnp.arange(n_row, dtype=jnp.int32)
    row_pick = (~is_col)[..., None] & (pull[..., None] == shifts)
    row_push = (~is_col)[..., None] & (push[..., None] == shifts)
    forward = []
    for height in range(levels):
        target = top_right[height] - updates[height]
        if height > 0:
            picked = gather_sources(forward[-1], col_pick[height - 1], row_pick[height - 1])
            target = target - jnp.einsum(
                "jrs,jts->rt", picked, top_blocks[height - 1], precision=highest
            )
        forward.append(apply_inverse(top_inverse[height], target))
    forward = jnp.stack(forward)
    current = apply_transpose(top_inverse[levels - 1], forward[levels - 1])
    solved = jnp.zeros_like(forward).at[levels - 1].set(current)

    def step(i, carry):
        current, solved = carry
        height = levels - 2 - i
        at = lambda a: lax.dynamic_index_in_dim(a, height, 0, keepdims=False)
        pieces = jnp.einsum("rt,jts->jrs", current, at(top_blocks), precision=highest)
        incoming = push_back(pieces, at(col_pick), at(row_push))
        current = apply_transpose(at(top_inverse), at(forward) - incoming)
        return (current, lax.dynamic_update_index_in_dim(solved, current, height, 0))

    return lax.fori_loop(0, levels - 1, step, (current, solved))[1]


def on_device(local_inv, local_off, local_dep, local_rhs, top_inv, top_off, top_dep, top_rhs):
    inverse = local_inv[0, 0]
    blocks = local_off[0, 0]
    ancestor_levels = local_dep[0, 0]
    right_local = local_rhs[0, 0]
    levels = top_inv.shape[0]
    top_inverse = top_inv[:, 0, 0]
    top_blocks = top_off[:, 0, 0]
    top_links = top_dep[:, 0, 0]
    top_right = top_rhs[:, 0, 0]
    local_first = jnp.einsum("krs,kts->krt", right_local, inverse, precision=highest)
    contributions = jnp.einsum("krs,kjts->kjrt", local_first, blocks, precision=highest)
    level_matches = (ancestor_levels[:, :, None] == jnp.arange(levels, dtype=jnp.int32)).astype(
        jnp.float32
    )
    updates = jnp.einsum("kjl,kjrt->lrt", level_matches, contributions, precision=highest)
    n_leaf = lax.axis_size("leaf")
    by_shift = jnp.stack([updates] + [shifted(updates, "leaf", k) for k in range(1, n_leaf)])
    order = jnp.mod(lax.axis_index("leaf") - jnp.arange(n_leaf, dtype=jnp.int32), n_leaf)
    weights = order[:, None] == jnp.arange(n_leaf, dtype=jnp.int32)
    ordered = select_sum(weights, by_shift)
    totals = ordered[0]
    for u in range(1, n_leaf):
        totals = totals + ordered[u]
    top_solution = solve_top(top_inverse, top_blocks, top_links, top_right, totals)
    ancestors = jnp.einsum("kjl,lrt->kjrt", level_matches, top_solution, precision=highest)
    remainder = local_first - jnp.einsum("kjrt,kjts->krs", ancestors, blocks, precision=highest)
    local_solution = jnp.einsum("krs,kst->krt", remainder, inverse, precision=highest)
    return (local_solution[None, None], top_solution[:, None, None])


def solution(mesh):
    placed = (
        P("leaf", "row", "col", None, None),
        P("leaf", "row", "col", None, None, None),
        P("leaf", "row", "col", None),
        P("leaf", "row", "col", None, None),
        P(None, "row", "col", None, None),
        P(None, "row", "col", None, None, None),
        P(None, "row", "col", None),
        P(None, "row", "col", None, None),
    )
    return jax.shard_map(
        on_device,
        mesh=mesh,
        in_specs=placed,
        out_specs=(P("leaf", "row", "col", None, None), P(None, "row", "col", None, None)),
        check_vma=False,
    )
```

profile of v0, /device:TPU:1, one launch (start us, length us, event | category | flops | bytes accessed | tf_op | source)
XLA Modules:
  0.0 378.8 jit_solution(4697018135431169076)
XLA Ops:
  0.6 3.7 fusion.36
  14.9 8.8 %collective-permute-done.4 = f32[8,64,128]{2,0,1:T(8,128)S(1)} collective-permute-done((f32[8,64,128]{2,0,1:T(8,128)S(1)}, f32[8,64,128]{2,0,1:T(8,128)S(1)}, u32[]{:S(2)}, u32[]{:S(2)}) %collective-permute-start.4) | collective-permute-done | bytes 262176 | tf_op jit(solution)/shard_map/ppermute | solution.py:19
  31.6 23.6 %all-gather = f32[1024,128]{1,0:T(8,128)S(1)} all-gather(f32[64,128]{1,0:T(8,128)S(1)} %get-tuple-element.254), channel_id=2, replica_groups=mesh['leaf'=4,'row'=4,'col'=16] {'col'}, dimensions={0}, use_global_device_ids=true | all-gather | bytes 557056 | tf_op jit(solution)/shard_map/all_gather | solution.py:32
  61.0 16.3 %all-gather.1 = f32[1024,128]{1,0:T(8,128)S(1)} all-gather(f32[64,128]{1,0:T(8,128)S(1)} %get-tuple-element.256), channel_id=3, replica_groups=mesh['leaf'=4,'row'=4,'col'=16] {'col'}, dimensions={0}, use_global_device_ids=true | all-gather | bytes 557056 | tf_op jit(solution)/shard_map/all_gather | solution.py:32
  84.7 18.2 %all-gather.2 = f32[1024,128]{1,0:T(8,128)S(1)} all-gather(f32[64,128]{1,0:T(8,128)S(1)} %get-tuple-element.258), channel_id=4, replica_groups=mesh['leaf'=4,'row'=4,'col'=16] {'col'}, dimensions={0}, use_global_device_ids=true | all-gather | bytes 557056 | tf_op jit(solution)/shard_map/all_gather | solution.py:32
  108.5 16.5 %all-gather.3 = f32[1024,128]{1,0:T(8,128)S(1)} all-gather(f32[64,128]{1,0:T(8,128)S(1)} %get-tuple-element.260), channel_id=5, replica_groups=mesh['leaf'=4,'row'=4,'col'=16] {'col'}, dimensions={0}, use_global_device_ids=true | all-gather | bytes 557056 | tf_op jit(solution)/shard_map/all_gather | solution.py:32
  132.4 18.2 %all-gather.4 = f32[1024,128]{1,0:T(8,128)S(1)} all-gather(f32[64,128]{1,0:T(8,128)S(1)} %get-tuple-element.262), channel_id=6, replica_groups=mesh['leaf'=4,'row'=4,'col'=16] {'col'}, dimensions={0}, use_global_device_ids=true | all-gather | bytes 557056 | tf_op jit(solution)/shard_map/all_gather | solution.py:32
  156.3 16.7 %all-gather.5 = f32[1024,128]{1,0:T(8,128)S(1)} all-gather(f32[64,128]{1,0:T(8,128)S(1)} %get-tuple-element.264), channel_id=7, replica_groups=mesh['leaf'=4,'row'=4,'col'=16] {'col'}, dimensions={0}, use_global_device_ids=true | all-gather | bytes 557056 | tf_op jit(solution)/shard_map/all_gather | solution.py:32
  180.4 18.2 %all-gather.6 = f32[1024,128]{1,0:T(8,128)S(1)} all-gather(f32[64,128]{1,0:T(8,128)S(1)} %get-tuple-element.266), channel_id=8, replica_groups=mesh['leaf'=4,'row'=4,'col'=16] {'col'}, dimensions={0}, use_global_device_ids=true | all-gather | bytes 557056 | tf_op jit(solution)/shard_map/all_gather | solution.py:32
  203.3 170.0 %while.18 = (s32[]{:T(128)}, f32[64,128]{1,0:T(8,128)S(1)}, f32[8,64,128]{2,1,0:T(8,128)}, f32[8,64,128]{2,1,0:T(8,128)}, pred[7,4,16]{2,1,0:T(4,128)(4,1)S(1)},...) while((s32[]{:T(128)}, f32[64,128]{1,0:T(8,128)S(1)}, ...), condition=%wide.region_19.20_spmd, body=%wide.region_15.19_spmd.sunk | while | flops 64225288 | bytes 4393060 | solution.py:83
  205.5 3.8 %all-to-all-start = ((f32[16,64,128]{2,1,0:T(8,128)}), f32[16,64,128]{2,1,0:T(8,128)S(1)}, u32[]{:S(2)}, u32[]{:S(2)}) async-start(f32[16,64,128]{2,1,0:T(8,128)} %select_reduce_fusion.20), calls=%async_computation | async-start | bytes 1048576 | tf_op jit(solution)/shard_map/while/body/eval_jaxpr/all_to_all | solution.py:41
  211.0 15.5 %all-to-all-done = f32[16,64,128]{2,1,0:T(8,128)S(1)} async-done(((f32[16,64,128]{2,1,0:T(8,128)}), f32[16,64,128]{2,1,0:T(8,128)S(1)}, u32[]{:S(2)}, u32[]{:S(2)}) %all-to-all-start) | async-done | bytes 524320 | tf_op jit(solution)/shard_map/while/body/eval_jaxpr/all_to_all | solution.py:41
  230.5 3.5 all-to-all-start
  235.7 15.0 %all-to-all-done = f32[16,64,128]{2,1,0:T(8,128)S(1)} async-done(((f32[16,64,128]{2,1,0:T(8,128)}), f32[16,64,128]{2,1,0:T(8,128)S(1)}, u32[]{:S(2)}, u32[]{:S(2)}) %all-to-all-start) | async-done | bytes 524320 | tf_op jit(solution)/shard_map/while/body/eval_jaxpr/all_to_all | solution.py:41
  254.7 3.5 all-to-all-start
  259.9 15.0 %all-to-all-done = f32[16,64,128]{2,1,0:T(8,128)S(1)} async-done(((f32[16,64,128]{2,1,0:T(8,128)}), f32[16,64,128]{2,1,0:T(8,128)S(1)}, u32[]{:S(2)}, u32[]{:S(2)}) %all-to-all-start) | async-done | bytes 524320 | tf_op jit(solution)/shard_map/while/body/eval_jaxpr/all_to_all | solution.py:41
  278.9 3.5 all-to-all-start
  284.0 15.0 %all-to-all-done = f32[16,64,128]{2,1,0:T(8,128)S(1)} async-done(((f32[16,64,128]{2,1,0:T(8,128)}), f32[16,64,128]{2,1,0:T(8,128)S(1)}, u32[]{:S(2)}, u32[]{:S(2)}) %all-to-all-start) | async-done | bytes 524320 | tf_op jit(solution)/shard_map/while/body/eval_jaxpr/all_to_all | solution.py:41
  303.0 3.5 all-to-all-start
  308.2 15.0 %all-to-all-done = f32[16,64,128]{2,1,0:T(8,128)S(1)} async-done(((f32[16,64,128]{2,1,0:T(8,128)}), f32[16,64,128]{2,1,0:T(8,128)S(1)}, u32[]{:S(2)}, u32[]{:S(2)}) %all-to-all-start) | async-done | bytes 524320 | tf_op jit(solution)/shard_map/while/body/eval_jaxpr/all_to_all | solution.py:41
  327.2 3.5 all-to-all-start
  332.4 15.0 %all-to-all-done = f32[16,64,128]{2,1,0:T(8,128)S(1)} async-done(((f32[16,64,128]{2,1,0:T(8,128)}), f32[16,64,128]{2,1,0:T(8,128)S(1)}, u32[]{:S(2)}, u32[]{:S(2)}) %all-to-all-start) | async-done | bytes 524320 | tf_op jit(solution)/shard_map/while/body/eval_jaxpr/all_to_all | solution.py:41
  351.4 3.5 all-to-all-start
  356.5 15.0 %all-to-all-done = f32[16,64,128]{2,1,0:T(8,128)S(1)} async-done(((f32[16,64,128]{2,1,0:T(8,128)}), f32[16,64,128]{2,1,0:T(8,128)S(1)}, u32[]{:S(2)}, u32[]{:S(2)}) %all-to-all-start) | async-done | bytes 524320 | tf_op jit(solution)/shard_map/while/body/eval_jaxpr/all_to_all | solution.py:41
  (216 shorter events, 106.5 us)
Async XLA Ops:
  26.5 28.9 %collective-permute-start.6 = (f32[64,128]{1,0:T(8,128)S(1)}, f32[64,128]{1,0:T(8,128)S(1)}, u32[]{:S(2)}, u32[]{:S(2)}) collective-permute-start(f32[64,128]{1,0:T(8,128)S(1)} %get-tuple-element.254), channel_id=1, source_target_pairs={{0,16},{16,32},{32,48},{48,0},{1,17},{17,33},{33,49},{49,1},{2,18}... | collective-permute-start | bytes 98312 | tf_op jit(solution)/shard_map/ppermute | solution.py:19
  27.9 27.5 %collective-permute-start.7 = (f32[64,128]{1,0:T(8,128)S(1)}, f32[64,128]{1,0:T(8,128)S(1)}, u32[]{:S(2)}, u32[]{:S(2)}) collective-permute-start(f32[64,128]{1,0:T(8,128)S(1)} %get-tuple-element.254), channel_id=1, source_target_pairs={{0,32},{16,48},{32,0},{48,16},{1,33},{17,49},{33,1},{49,17},{2,34}... | collective-permute-start | bytes 98312 | tf_op jit(solution)/shard_map/ppermute | solution.py:19
  30.5 24.9 %collective-permute-start.8 = (f32[64,128]{1,0:T(8,128)S(1)}, f32[64,128]{1,0:T(8,128)S(1)}, u32[]{:S(2)}, u32[]{:S(2)}) collective-permute-start(f32[64,128]{1,0:T(8,128)S(1)} %get-tuple-element.254), channel_id=1, source_target_pairs={{0,48},{16,0},{32,16},{48,32},{1,49},{17,1},{33,17},{49,33},{2,50}... | collective-permute-start | bytes 98312 | tf_op jit(solution)/shard_map/ppermute | solution.py:19
  58.1 19.5 %collective-permute-start.9 = (f32[64,128]{1,0:T(8,128)S(1)}, f32[64,128]{1,0:T(8,128)S(1)}, u32[]{:S(2)}, u32[]{:S(2)}) collective-permute-start(f32[64,128]{1,0:T(8,128)S(1)} %get-tuple-element.256), channel_id=1, source_target_pairs={{0,16},{16,32},{32,48},{48,0},{1,17},{17,33},{33,49},{49,1},{2,18}... | collective-permute-start | bytes 98312 | tf_op jit(solution)/shard_map/ppermute | solution.py:19
  80.1 23.0 %collective-permute-start.12 = (f32[64,128]{1,0:T(8,128)S(1)}, f32[64,128]{1,0:T(8,128)S(1)}, u32[]{:S(2)}, u32[]{:S(2)}) collective-permute-start(f32[64,128]{1,0:T(8,128)S(1)} %get-tuple-element.258), channel_id=1, source_target_pairs={{0,16},{16,32},{32,48},{48,0},{1,17},{17,33},{33,49},{49,1},{2,18}... | collective-permute-start | bytes 98312 | tf_op jit(solution)/shard_map/ppermute | solution.py:19
  80.6 22.6 %collective-permute-start.13 = (f32[64,128]{1,0:T(8,128)S(1)}, f32[64,128]{1,0:T(8,128)S(1)}, u32[]{:S(2)}, u32[]{:S(2)}) collective-permute-start(f32[64,128]{1,0:T(8,128)S(1)} %get-tuple-element.258), channel_id=1, source_target_pairs={{0,32},{16,48},{32,0},{48,16},{1,33},{17,49},{33,1},{49,17},{2,34}... | collective-permute-start | bytes 98312 | tf_op jit(solution)/shard_map/ppermute | solution.py:19
  82.7 20.4 %collective-permute-start.14 = (f32[64,128]{1,0:T(8,128)S(1)}, f32[64,128]{1,0:T(8,128)S(1)}, u32[]{:S(2)}, u32[]{:S(2)}) collective-permute-start(f32[64,128]{1,0:T(8,128)S(1)} %get-tuple-element.258), channel_id=1, source_target_pairs={{0,48},{16,0},{32,16},{48,32},{1,49},{17,1},{33,17},{49,33},{2,50}... | collective-permute-start | bytes 98312 | tf_op jit(solution)/shard_map/ppermute | solution.py:19
  105.8 19.5 %collective-permute-start.15 = (f32[64,128]{1,0:T(8,128)S(1)}, f32[64,128]{1,0:T(8,128)S(1)}, u32[]{:S(2)}, u32[]{:S(2)}) collective-permute-start(f32[64,128]{1,0:T(8,128)S(1)} %get-tuple-element.260), channel_id=1, source_target_pairs={{0,16},{16,32},{32,48},{48,0},{1,17},{17,33},{33,49},{49,1},{2,18}... | collective-permute-start | bytes 98312 | tf_op jit(solution)/shard_map/ppermute | solution.py:19
  105.9 19.4 %collective-permute-start.16 = (f32[64,128]{1,0:T(8,128)S(1)}, f32[64,128]{1,0:T(8,128)S(1)}, u32[]{:S(2)}, u32[]{:S(2)}) collective-permute-start(f32[64,128]{1,0:T(8,128)S(1)} %get-tuple-element.260), channel_id=1, source_target_pairs={{0,32},{16,48},{32,0},{48,16},{1,33},{17,49},{33,1},{49,17},{2,34}... | collective-permute-start | bytes 98312 | tf_op jit(solution)/shard_map/ppermute | solution.py:19
  127.9 23.0 %collective-permute-start.18 = (f32[64,128]{1,0:T(8,128)S(1)}, f32[64,128]{1,0:T(8,128)S(1)}, u32[]{:S(2)}, u32[]{:S(2)}) collective-permute-start(f32[64,128]{1,0:T(8,128)S(1)} %get-tuple-element.262), channel_id=1, source_target_pairs={{0,16},{16,32},{32,48},{48,0},{1,17},{17,33},{33,49},{49,1},{2,18}... | collective-permute-start | bytes 98312 | tf_op jit(solution)/shard_map/ppermute | solution.py:19
  128.3 22.6 %collective-permute-start.19 = (f32[64,128]{1,0:T(8,128)S(1)}, f32[64,128]{1,0:T(8,128)S(1)}, u32[]{:S(2)}, u32[]{:S(2)}) collective-permute-start(f32[64,128]{1,0:T(8,128)S(1)} %get-tuple-element.262), channel_id=1, source_target_pairs={{0,32},{16,48},{32,0},{48,16},{1,33},{17,49},{33,1},{49,17},{2,34}... | collective-permute-start | bytes 98312 | tf_op jit(solution)/shard_map/ppermute | solution.py:19
  130.5 20.4 %collective-permute-start.20 = (f32[64,128]{1,0:T(8,128)S(1)}, f32[64,128]{1,0:T(8,128)S(1)}, u32[]{:S(2)}, u32[]{:S(2)}) collective-permute-start(f32[64,128]{1,0:T(8,128)S(1)} %get-tuple-element.262), channel_id=1, source_target_pairs={{0,48},{16,0},{32,16},{48,32},{1,49},{17,1},{33,17},{49,33},{2,50}... | collective-permute-start | bytes 98312 | tf_op jit(solution)/shard_map/ppermute | solution.py:19
  153.5 19.7 %collective-permute-start.21 = (f32[64,128]{1,0:T(8,128)S(1)}, f32[64,128]{1,0:T(8,128)S(1)}, u32[]{:S(2)}, u32[]{:S(2)}) collective-permute-start(f32[64,128]{1,0:T(8,128)S(1)} %get-tuple-element.264), channel_id=1, source_target_pairs={{0,16},{16,32},{32,48},{48,0},{1,17},{17,33},{33,49},{49,1},{2,18}... | collective-permute-start | bytes 98312 | tf_op jit(solution)/shard_map/ppermute | solution.py:19
  153.6 19.6 %collective-permute-start.22 = (f32[64,128]{1,0:T(8,128)S(1)}, f32[64,128]{1,0:T(8,128)S(1)}, u32[]{:S(2)}, u32[]{:S(2)}) collective-permute-start(f32[64,128]{1,0:T(8,128)S(1)} %get-tuple-element.264), channel_id=1, source_target_pairs={{0,32},{16,48},{32,0},{48,16},{1,33},{17,49},{33,1},{49,17},{2,34}... | collective-permute-start | bytes 98312 | tf_op jit(solution)/shard_map/ppermute | solution.py:19
  175.8 23.0 %collective-permute-start.24 = (f32[64,128]{1,0:T(8,128)S(1)}, f32[64,128]{1,0:T(8,128)S(1)}, u32[]{:S(2)}, u32[]{:S(2)}) collective-permute-start(f32[64,128]{1,0:T(8,128)S(1)} %get-tuple-element.266), channel_id=1, source_target_pairs={{0,16},{16,32},{32,48},{48,0},{1,17},{17,33},{33,49},{49,1},{2,18}... | collective-permute-start | bytes 98312 | tf_op jit(solution)/shard_map/ppermute | solution.py:19
  176.2 22.6 %collective-permute-start.25 = (f32[64,128]{1,0:T(8,128)S(1)}, f32[64,128]{1,0:T(8,128)S(1)}, u32[]{:S(2)}, u32[]{:S(2)}) collective-permute-start(f32[64,128]{1,0:T(8,128)S(1)} %get-tuple-element.266), channel_id=1, source_target_pairs={{0,32},{16,48},{32,0},{48,16},{1,33},{17,49},{33,1},{49,17},{2,34}... | collective-permute-start | bytes 98312 | tf_op jit(solution)/shard_map/ppermute | solution.py:19
  178.4 20.4 %collective-permute-start.26 = (f32[64,128]{1,0:T(8,128)S(1)}, f32[64,128]{1,0:T(8,128)S(1)}, u32[]{:S(2)}, u32[]{:S(2)}) collective-permute-start(f32[64,128]{1,0:T(8,128)S(1)} %get-tuple-element.266), channel_id=1, source_target_pairs={{0,48},{16,0},{32,16},{48,32},{1,49},{17,1},{33,17},{49,33},{2,50}... | collective-permute-start | bytes 98312 | tf_op jit(solution)/shard_map/ppermute | solution.py:19
  205.5 21.0 %all-to-all-start = ((f32[16,64,128]{2,1,0:T(8,128)}), f32[16,64,128]{2,1,0:T(8,128)S(1)}, u32[]{:S(2)}, u32[]{:S(2)}) async-start(f32[16,64,128]{2,1,0:T(8,128)} %select_reduce_fusion.20), calls=%async_computation | async-start | bytes 1048576 | tf_op jit(solution)/shard_map/while/body/eval_jaxpr/all_to_all | solution.py:41
  230.5 20.2 %all-to-all-start = ((f32[16,64,128]{2,1,0:T(8,128)}), f32[16,64,128]{2,1,0:T(8,128)S(1)}, u32[]{:S(2)}, u32[]{:S(2)}) async-start(f32[16,64,128]{2,1,0:T(8,128)} %select_reduce_fusion.20), calls=%async_computation | async-start | bytes 1048576 | tf_op jit(solution)/shard_map/while/body/eval_jaxpr/all_to_all | solution.py:41
  254.7 20.2 %all-to-all-start = ((f32[16,64,128]{2,1,0:T(8,128)}), f32[16,64,128]{2,1,0:T(8,128)S(1)}, u32[]{:S(2)}, u32[]{:S(2)}) async-start(f32[16,64,128]{2,1,0:T(8,128)} %select_reduce_fusion.20), calls=%async_computation | async-start | bytes 1048576 | tf_op jit(solution)/shard_map/while/body/eval_jaxpr/all_to_all | solution.py:41
  278.9 20.2 %all-to-all-start = ((f32[16,64,128]{2,1,0:T(8,128)}), f32[16,64,128]{2,1,0:T(8,128)S(1)}, u32[]{:S(2)}, u32[]{:S(2)}) async-start(f32[16,64,128]{2,1,0:T(8,128)} %select_reduce_fusion.20), calls=%async_computation | async-start | bytes 1048576 | tf_op jit(solution)/shard_map/while/body/eval_jaxpr/all_to_all | solution.py:41
  303.0 20.2 %all-to-all-start = ((f32[16,64,128]{2,1,0:T(8,128)}), f32[16,64,128]{2,1,0:T(8,128)S(1)}, u32[]{:S(2)}, u32[]{:S(2)}) async-start(f32[16,64,128]{2,1,0:T(8,128)} %select_reduce_fusion.20), calls=%async_computation | async-start | bytes 1048576 | tf_op jit(solution)/shard_map/while/body/eval_jaxpr/all_to_all | solution.py:41
  327.2 20.2 %all-to-all-start = ((f32[16,64,128]{2,1,0:T(8,128)}), f32[16,64,128]{2,1,0:T(8,128)S(1)}, u32[]{:S(2)}, u32[]{:S(2)}) async-start(f32[16,64,128]{2,1,0:T(8,128)} %select_reduce_fusion.20), calls=%async_computation | async-start | bytes 1048576 | tf_op jit(solution)/shard_map/while/body/eval_jaxpr/all_to_all | solution.py:41
  351.4 20.2 %all-to-all-start = ((f32[16,64,128]{2,1,0:T(8,128)}), f32[16,64,128]{2,1,0:T(8,128)S(1)}, u32[]{:S(2)}, u32[]{:S(2)}) async-start(f32[16,64,128]{2,1,0:T(8,128)} %select_reduce_fusion.20), calls=%async_computation | async-start | bytes 1048576 | tf_op jit(solution)/shard_map/while/body/eval_jaxpr/all_to_all | solution.py:41
  (34 other events, 498.5 us)
where the time goes:
time: 381 us; the launch traced here: 379 us
  blocking collectives  128 us (34%)
  waiting for transfers between devices  115 us (30%)
  starting transfers between devices  68.4 us (18%)
  matrix products  52.2 us (14%)
  other arithmetic  11.9 us (3%)
    all_gather x7, blocking collectives, gather_sources(): by_col = lax.all_gather(block[None], 'col', axis=0, tiled=True)  128 us
    all_to_all x7, waiting for transfers between devices, push_back(): incoming = lax.all_to_all(slots, 'col', 0, 0, tiled=True).sum(0)  106 us
    ppermute x45, starting transfers between devices, shifted(): return lax.ppermute(value, axis, [(i, (i + k) % n) for i in range(n)])  43.7 us
    all_to_all x7, starting transfers between devices, push_back(): incoming = lax.all_to_all(slots, 'col', 0, 0, tiled=True).sum(0)  24.6 us
    dot_general x8, matrix products, apply_transpose(): return jnp.einsum('rs,st->rt', block, inverse, precision=highest)  12.8 us
    ppermute x45, waiting for transfers between devices, shifted(): return lax.ppermute(value, axis, [(i, (i + k) % n) for i in range(n)])  9.6 us
    dot_general x7, matrix products, solve_top(): jnp.einsum('jrs,jts->rt', picked, top_blocks[height - 1], precision=highest)  9.58 us
    dot_general x8, matrix products, apply_inverse(): return jnp.einsum('rs,ts->rt', block, inverse, precision=highest)  8.76 us
  transfers between devices with their start and end apart: 52, of which 9 were waited for; matrix products, arithmetic and copies ran while one was open for 1% of the time, Pallas kernels for 0%

commit v1 on v0

--- a/solution.py
+++ b/solution.py
@@ -4,6 +4,12 @@
 from jax.sharding import PartitionSpec as P
 
 highest = lax.Precision.HIGHEST
+
+
+def laid_out(blocks, dim):
+    dims = list(blocks.shape[1:])
+    dims[dim] *= blocks.shape[0]
+    return jnp.moveaxis(blocks, 0, dim).reshape(dims)
 
 
 def apply_inverse(inverse, block):
@@ -29,7 +35,19 @@
 
 
 def gather_sources(block, col_pick, row_pick):
-    by_col = lax.all_gather(block[None], "col", axis=0, tiled=True)
+    size = lax.axis_size("col")
+    pairs = [(i_2, (i_2 + 1) % size) for i_2 in range(size)]
+    back = [(b, a_2) for a_2, b in pairs]
+    lower, upper = ([], [])
+    for step_2 in range(size - 1):
+        if step_2 % 2 == 0:
+            lower.append(lax.ppermute(lower[-1] if lower else block[None], "col", pairs))
+        else:
+            upper.append(lax.ppermute(upper[-1] if upper else block[None], "col", back))
+    blocks_2 = jnp.stack([*lower[::-1], block[None], *upper])
+    shift = lax.axis_index("col") - len(lower)
+    blocks_2 = blocks_2[(jnp.arange(size) - shift) % size]
+    by_col = laid_out(blocks_2, 0)
     n_row = lax.axis_size("row")
     by_shift = jnp.stack([block] + [shifted(block, "row", k) for k in range(1, n_row)])
     return select_sum(col_pick, by_col) + select_sum(row_pick, by_shift)

time: 381 us -> 548 us (1.44); the launches traced: 379 us -> 537 us
  starting transfers between devices: 68.4 us -> 263 us
  blocking collectives: 128 us -> 0 us
  waiting for transfers between devices: 115 us -> 174 us
  local copies, waits for them, and re-layouts: 1.48 us -> 20.1 us
  other arithmetic: 11.9 us -> 20.9 us
    ppermute x0 -> x105, starting transfers between devices: none -> 186 us  [the longest x49 179 us: gather_sources(): upper.append(lax.ppermute(upper[-1] if upper else block[None], 'col', back))]
    all_gather x7 -> x0, blocking collectives: 128 us -> none  [gather_sources(): by_col = lax.all_gather(block[None], 'col', axis=0, tiled=True)]
    ppermute x0 -> x105, waiting for transfers between devices: none -> 59.6 us  [the longest x56 44.6 us: gather_sources(): lax.ppermute(lower[-1] if lower else block[None], 'col', pairs)]
    gather x0 -> x7, local copies, waits for them, and re-layouts: none -> 11.3 us  [gather_sources(): blocks_2 = blocks_2[(jnp.arange(size) - shift) % size]]
    reduce_sum x15, other arithmetic: 2.55 us -> 11.5 us  [select_sum(): return jnp.sum(jnp.where(mask, stacked[None], 0.0), axis=1)]
    all_to_all x7, starting transfers between devices: 24.6 us -> 31.7 us  [push_back(): incoming = lax.all_to_all(slots, 'col', 0, 0, tiled=True).sum(0)]
    unnamed x12 -> x127, local copies, waits for them, and re-layouts: 0.04 us -> 6.1 us
  transfers between devices with their start and end apart: 52 -> 157, of which waited for: 9 -> 83; matrix products, arithmetic and copies ran while one was open for 1% -> 2% of each run, Pallas kernels for 0% -> 0%
where the time goes in v1:
time: 548 us; the launch traced here: 537 us
  starting transfers between devices  263 us (48%)
  waiting for transfers between devices  174 us (32%)
  matrix products  56.8 us (10%)
  other arithmetic  20.9 us (4%)
  local copies, waits for them, and re-layouts  20.1 us (4%)
    ppermute x49, starting transfers between devices, gather_sources(): upper.append(lax.ppermute(upper[-1] if upper else block[None], 'col', back))  179 us
    all_to_all x7, waiting for transfers between devices, push_back(): incoming = lax.all_to_all(slots, 'col', 0, 0, tiled=True).sum(0)  105 us
    ppermute x56, waiting for transfers between devices, gather_sources(): lax.ppermute(lower[-1] if lower else block[None], 'col', pairs)  44.6 us
    ppermute x45, starting transfers between devices, shifted(): return lax.ppermute(value, axis, [(i, (i + k) % n) for i in range(n)])  44.5 us
    all_to_all x7, starting transfers between devices, push_back(): incoming = lax.all_to_all(slots, 'col', 0, 0, tiled=True).sum(0)  31.7 us
    ppermute x49, waiting for transfers between devices, gather_sources(): upper.append(lax.ppermute(upper[-1] if upper else block[None], 'col', back))  15 us
    dot_general x8, matrix products, apply_inverse(): return jnp.einsum('rs,ts->rt', block, inverse, precision=highest)  13.6 us
    dot_general x8, matrix products, apply_transpose(): return jnp.einsum('rs,st->rt', block, inverse, precision=highest)  12.7 us
  transfers between devices with their start and end apart: 157, of which 83 were waited for; matrix products, arithmetic and copies ran while one was open for 2% of the time, Pallas kernels for 0%

profile of v1, /device:TPU:1, one launch (start us, length us, event | category | flops | bytes accessed | tf_op | source)
XLA Modules:
  0.0 537.5 jit_solution(137293827724823548)
XLA Ops:
  14.9 8.8 %collective-permute-done.4 = f32[8,64,128]{2,0,1:T(8,128)S(1)} collective-permute-done((f32[8,64,128]{2,0,1:T(8,128)S(1)}, f32[8,64,128]{2,0,1:T(8,128)S(1)}, u32[]{:S(2)}, u32[]{:S(2)}) %collective-permute-start.4) | collective-permute-done | bytes 262176 | tf_op jit(solution)/shard_map/ppermute | solution.py:25
  49.5 4.7 collective-permute-start.17
  74.2 4.4 collective-permute-done.24
  100.1 4.4 collective-permute-start.36
  120.2 4.4 collective-permute-done.42
  147.1 4.7 collective-permute-start.54
  167.2 4.4 collective-permute-done.60
  171.6 3.9 collective-permute-start.68
  192.6 4.7 collective-permute-start.72
  212.8 4.4 collective-permute-done.78
  239.8 4.7 collective-permute-start.90
  259.9 4.4 collective-permute-done.96
  285.4 4.7 collective-permute-start.108
  305.7 4.4 collective-permute-done.114
  332.8 4.7 collective-permute-start.126
  354.7 177.1 %while.18 = (s32[]{:T(128)}, f32[64,128]{1,0:T(8,128)S(1)}, f32[8,64,128]{2,1,0:T(8,128)}, f32[8,64,128]{2,1,0:T(8,128)}, pred[7,4,16]{2,1,0:T(4,128)(4,1)S(1)},...) while((s32[]{:T(128)}, f32[64,128]{1,0:T(8,128)S(1)}, ...), condition=%wide.region_19.20_spmd, body=%wide.region_15.19_spmd.sunk | while | flops 64225288 | bytes 4393060 | solution.py:101
  356.9 10.9 %all-to-all-start = ((f32[16,64,128]{2,1,0:T(8,128)}), f32[16,64,128]{2,1,0:T(8,128)S(1)}, u32[]{:S(2)}, u32[]{:S(2)}) async-start(f32[16,64,128]{2,1,0:T(8,128)} %select_reduce_fusion.20), calls=%async_computation | async-start | bytes 1048576 | tf_op jit(solution)/shard_map/while/body/eval_jaxpr/all_to_all | solution.py:59
  369.6 15.4 %all-to-all-done = f32[16,64,128]{2,1,0:T(8,128)S(1)} async-done(((f32[16,64,128]{2,1,0:T(8,128)}), f32[16,64,128]{2,1,0:T(8,128)S(1)}, u32[]{:S(2)}, u32[]{:S(2)}) %all-to-all-start) | async-done | bytes 524320 | tf_op jit(solution)/shard_map/while/body/eval_jaxpr/all_to_all | solution.py:59
  394.3 14.9 %all-to-all-done = f32[16,64,128]{2,1,0:T(8,128)S(1)} async-done(((f32[16,64,128]{2,1,0:T(8,128)}), f32[16,64,128]{2,1,0:T(8,128)S(1)}, u32[]{:S(2)}, u32[]{:S(2)}) %all-to-all-start) | async-done | bytes 524320 | tf_op jit(solution)/shard_map/while/body/eval_jaxpr/all_to_all | solution.py:59
  418.5 14.9 %all-to-all-done = f32[16,64,128]{2,1,0:T(8,128)S(1)} async-done(((f32[16,64,128]{2,1,0:T(8,128)}), f32[16,64,128]{2,1,0:T(8,128)S(1)}, u32[]{:S(2)}, u32[]{:S(2)}) %all-to-all-start) | async-done | bytes 524320 | tf_op jit(solution)/shard_map/while/body/eval_jaxpr/all_to_all | solution.py:59
  442.6 14.9 %all-to-all-done = f32[16,64,128]{2,1,0:T(8,128)S(1)} async-done(((f32[16,64,128]{2,1,0:T(8,128)}), f32[16,64,128]{2,1,0:T(8,128)S(1)}, u32[]{:S(2)}, u32[]{:S(2)}) %all-to-all-start) | async-done | bytes 524320 | tf_op jit(solution)/shard_map/while/body/eval_jaxpr/all_to_all | solution.py:59
  466.8 14.9 %all-to-all-done = f32[16,64,128]{2,1,0:T(8,128)S(1)} async-done(((f32[16,64,128]{2,1,0:T(8,128)}), f32[16,64,128]{2,1,0:T(8,128)S(1)}, u32[]{:S(2)}, u32[]{:S(2)}) %all-to-all-start) | async-done | bytes 524320 | tf_op jit(solution)/shard_map/while/body/eval_jaxpr/all_to_all | solution.py:59
  491.0 14.9 %all-to-all-done = f32[16,64,128]{2,1,0:T(8,128)S(1)} async-done(((f32[16,64,128]{2,1,0:T(8,128)}), f32[16,64,128]{2,1,0:T(8,128)S(1)}, u32[]{:S(2)}, u32[]{:S(2)}) %all-to-all-start) | async-done | bytes 524320 | tf_op jit(solution)/shard_map/while/body/eval_jaxpr/all_to_all | solution.py:59
  515.2 14.9 %all-to-all-done = f32[16,64,128]{2,1,0:T(8,128)S(1)} async-done(((f32[16,64,128]{2,1,0:T(8,128)}), f32[16,64,128]{2,1,0:T(8,128)S(1)}, u32[]{:S(2)}, u32[]{:S(2)}) %all-to-all-start) | async-done | bytes 524320 | tf_op jit(solution)/shard_map/while/body/eval_jaxpr/all_to_all | solution.py:59
  (550 shorter events, 347.4 us)
Async XLA Ops:
  356.9 28.1 %all-to-all-start = ((f32[16,64,128]{2,1,0:T(8,128)}), f32[16,64,128]{2,1,0:T(8,128)S(1)}, u32[]{:S(2)}, u32[]{:S(2)}) async-start(f32[16,64,128]{2,1,0:T(8,128)} %select_reduce_fusion.20), calls=%async_computation | async-start | bytes 1048576 | tf_op jit(solution)/shard_map/while/body/eval_jaxpr/all_to_all | solution.py:59
  368.0 17.1 %collective-permute-start = (f32[64,128]{1,0:T(8,128)S(1)}, f32[64,128]{1,0:T(8,128)S(1)}, u32[]{:S(2)}, u32[]{:S(2)}) collective-permute-start(f32[64,128]{1,0:T(8,128)S(1)} %get-tuple-element.323), channel_id=1, source_target_pairs={{0,48},{16,0},{32,16},{48,32},{1,49},{17,1},{33,17},{49,33},{2,50}... | collective-permute-start | bytes 98312 | tf_op jit(solution)/shard_map/while/body/eval_jaxpr/ppermute | solution.py:25
  368.1 17.0 %collective-permute-start.1 = (f32[64,128]{1,0:T(8,128)S(1)}, f32[64,128]{1,0:T(8,128)S(1)}, u32[]{:S(2)}, u32[]{:S(2)}) collective-permute-start(f32[64,128]{1,0:T(8,128)S(1)} %get-tuple-element.324), channel_id=1, source_target_pairs={{0,32},{16,48},{32,0},{48,16},{1,33},{17,49},{33,1},{49,17},{2,34}... | collective-permute-start | bytes 98312 | tf_op jit(solution)/shard_map/while/body/eval_jaxpr/ppermute | solution.py:25
  369.2 15.9 %collective-permute-start.2 = (f32[64,128]{1,0:T(8,128)S(1)}, f32[64,128]{1,0:T(8,128)S(1)}, u32[]{:S(2)}, u32[]{:S(2)}) collective-permute-start(f32[64,128]{1,0:T(8,128)S(1)} %get-tuple-element.325), channel_id=1, source_target_pairs={{0,16},{16,32},{32,48},{48,0},{1,17},{17,33},{33,49},{49,1},{2,18}... | collective-permute-start | bytes 98312 | tf_op jit(solution)/shard_map/while/body/eval_jaxpr/ppermute | solution.py:25
  389.0 20.2 %all-to-all-start = ((f32[16,64,128]{2,1,0:T(8,128)}), f32[16,64,128]{2,1,0:T(8,128)S(1)}, u32[]{:S(2)}, u32[]{:S(2)}) async-start(f32[16,64,128]{2,1,0:T(8,128)} %select_reduce_fusion.20), calls=%async_computation | async-start | bytes 1048576 | tf_op jit(solution)/shard_map/while/body/eval_jaxpr/all_to_all | solution.py:59
  392.7 16.6 %collective-permute-start = (f32[64,128]{1,0:T(8,128)S(1)}, f32[64,128]{1,0:T(8,128)S(1)}, u32[]{:S(2)}, u32[]{:S(2)}) collective-permute-start(f32[64,128]{1,0:T(8,128)S(1)} %get-tuple-element.323), channel_id=1, source_target_pairs={{0,48},{16,0},{32,16},{48,32},{1,49},{17,1},{33,17},{49,33},{2,50}... | collective-permute-start | bytes 98312 | tf_op jit(solution)/shard_map/while/body/eval_jaxpr/ppermute | solution.py:25
  392.8 16.5 %collective-permute-start.1 = (f32[64,128]{1,0:T(8,128)S(1)}, f32[64,128]{1,0:T(8,128)S(1)}, u32[]{:S(2)}, u32[]{:S(2)}) collective-permute-start(f32[64,128]{1,0:T(8,128)S(1)} %get-tuple-element.324), channel_id=1, source_target_pairs={{0,32},{16,48},{32,0},{48,16},{1,33},{17,49},{33,1},{49,17},{2,34}... | collective-permute-start | bytes 98312 | tf_op jit(solution)/shard_map/while/body/eval_jaxpr/ppermute | solution.py:25
  413.2 20.2 %all-to-all-start = ((f32[16,64,128]{2,1,0:T(8,128)}), f32[16,64,128]{2,1,0:T(8,128)S(1)}, u32[]{:S(2)}, u32[]{:S(2)}) async-start(f32[16,64,128]{2,1,0:T(8,128)} %select_reduce_fusion.20), calls=%async_computation | async-start | bytes 1048576 | tf_op jit(solution)/shard_map/while/body/eval_jaxpr/all_to_all | solution.py:59
  416.8 16.6 %collective-permute-start = (f32[64,128]{1,0:T(8,128)S(1)}, f32[64,128]{1,0:T(8,128)S(1)}, u32[]{:S(2)}, u32[]{:S(2)}) collective-permute-start(f32[64,128]{1,0:T(8,128)S(1)} %get-tuple-element.323), channel_id=1, source_target_pairs={{0,48},{16,0},{32,16},{48,32},{1,49},{17,1},{33,17},{49,33},{2,50}... | collective-permute-start | bytes 98312 | tf_op jit(solution)/shard_map/while/body/eval_jaxpr/ppermute | solution.py:25
  416.9 16.5 %collective-permute-start.1 = (f32[64,128]{1,0:T(8,128)S(1)}, f32[64,128]{1,0:T(8,128)S(1)}, u32[]{:S(2)}, u32[]{:S(2)}) collective-permute-start(f32[64,128]{1,0:T(8,128)S(1)} %get-tuple-element.324), channel_id=1, source_target_pairs={{0,32},{16,48},{32,0},{48,16},{1,33},{17,49},{33,1},{49,17},{2,34}... | collective-permute-start | bytes 98312 | tf_op jit(solution)/shard_map/while/body/eval_jaxpr/ppermute | solution.py:25
  418.1 15.4 %collective-permute-start.2 = (f32[64,128]{1,0:T(8,128)S(1)}, f32[64,128]{1,0:T(8,128)S(1)}, u32[]{:S(2)}, u32[]{:S(2)}) collective-permute-start(f32[64,128]{1,0:T(8,128)S(1)} %get-tuple-element.325), channel_id=1, source_target_pairs={{0,16},{16,32},{32,48},{48,0},{1,17},{17,33},{33,49},{49,1},{2,18}... | collective-permute-start | bytes 98312 | tf_op jit(solution)/shard_map/while/body/eval_jaxpr/ppermute | solution.py:25
  437.4 20.2 %all-to-all-start = ((f32[16,64,128]{2,1,0:T(8,128)}), f32[16,64,128]{2,1,0:T(8,128)S(1)}, u32[]{:S(2)}, u32[]{:S(2)}) async-start(f32[16,64,128]{2,1,0:T(8,128)} %select_reduce_fusion.20), calls=%async_computation | async-start | bytes 1048576 | tf_op jit(solution)/shard_map/while/body/eval_jaxpr/all_to_all | solution.py:59
  441.0 16.6 %collective-permute-start = (f32[64,128]{1,0:T(8,128)S(1)}, f32[64,128]{1,0:T(8,128)S(1)}, u32[]{:S(2)}, u32[]{:S(2)}) collective-permute-start(f32[64,128]{1,0:T(8,128)S(1)} %get-tuple-element.323), channel_id=1, source_target_pairs={{0,48},{16,0},{32,16},{48,32},{1,49},{17,1},{33,17},{49,33},{2,50}... | collective-permute-start | bytes 98312 | tf_op jit(solution)/shard_map/while/body/eval_jaxpr/ppermute | solution.py:25
  441.1 16.5 %collective-permute-start.1 = (f32[64,128]{1,0:T(8,128)S(1)}, f32[64,128]{1,0:T(8,128)S(1)}, u32[]{:S(2)}, u32[]{:S(2)}) collective-permute-start(f32[64,128]{1,0:T(8,128)S(1)} %get-tuple-element.324), channel_id=1, source_target_pairs={{0,32},{16,48},{32,0},{48,16},{1,33},{17,49},{33,1},{49,17},{2,34}... | collective-permute-start | bytes 98312 | tf_op jit(solution)/shard_map/while/body/eval_jaxpr/ppermute | solution.py:25
  442.2 15.4 %collective-permute-start.2 = (f32[64,128]{1,0:T(8,128)S(1)}, f32[64,128]{1,0:T(8,128)S(1)}, u32[]{:S(2)}, u32[]{:S(2)}) collective-permute-start(f32[64,128]{1,0:T(8,128)S(1)} %get-tuple-element.325), channel_id=1, source_target_pairs={{0,16},{16,32},{32,48},{48,0},{1,17},{17,33},{33,49},{49,1},{2,18}... | collective-permute-start | bytes 98312 | tf_op jit(solution)/shard_map/while/body/eval_jaxpr/ppermute | solution.py:25
  461.5 20.2 %all-to-all-start = ((f32[16,64,128]{2,1,0:T(8,128)}), f32[16,64,128]{2,1,0:T(8,128)S(1)}, u32[]{:S(2)}, u32[]{:S(2)}) async-start(f32[16,64,128]{2,1,0:T(8,128)} %select_reduce_fusion.20), calls=%async_computation | async-start | bytes 1048576 | tf_op jit(solution)/shard_map/while/body/eval_jaxpr/all_to_all | solution.py:59
  465.1 16.6 %collective-permute-start = (f32[64,128]{1,0:T(8,128)S(1)}, f32[64,128]{1,0:T(8,128)S(1)}, u32[]{:S(2)}, u32[]{:S(2)}) collective-permute-start(f32[64,128]{1,0:T(8,128)S(1)} %get-tuple-element.323), channel_id=1, source_target_pairs={{0,48},{16,0},{32,16},{48,32},{1,49},{17,1},{33,17},{49,33},{2,50}... | collective-permute-start | bytes 98312 | tf_op jit(solution)/shard_map/while/body/eval_jaxpr/ppermute | solution.py:25
  465.3 16.5 %collective-permute-start.1 = (f32[64,128]{1,0:T(8,128)S(1)}, f32[64,128]{1,0:T(8,128)S(1)}, u32[]{:S(2)}, u32[]{:S(2)}) collective-permute-start(f32[64,128]{1,0:T(8,128)S(1)} %get-tuple-element.324), channel_id=1, source_target_pairs={{0,32},{16,48},{32,0},{48,16},{1,33},{17,49},{33,1},{49,17},{2,34}... | collective-permute-start | bytes 98312 | tf_op jit(solution)/shard_map/while/body/eval_jaxpr/ppermute | solution.py:25
  485.7 20.2 %all-to-all-start = ((f32[16,64,128]{2,1,0:T(8,128)}), f32[16,64,128]{2,1,0:T(8,128)S(1)}, u32[]{:S(2)}, u32[]{:S(2)}) async-start(f32[16,64,128]{2,1,0:T(8,128)} %select_reduce_fusion.20), calls=%async_computation | async-start | bytes 1048576 | tf_op jit(solution)/shard_map/while/body/eval_jaxpr/all_to_all | solution.py:59
  489.3 16.6 %collective-permute-start = (f32[64,128]{1,0:T(8,128)S(1)}, f32[64,128]{1,0:T(8,128)S(1)}, u32[]{:S(2)}, u32[]{:S(2)}) collective-permute-start(f32[64,128]{1,0:T(8,128)S(1)} %get-tuple-element.323), channel_id=1, source_target_pairs={{0,48},{16,0},{32,16},{48,32},{1,49},{17,1},{33,17},{49,33},{2,50}... | collective-permute-start | bytes 98312 | tf_op jit(solution)/shard_map/while/body/eval_jaxpr/ppermute | solution.py:25
  489.4 16.5 %collective-permute-start.1 = (f32[64,128]{1,0:T(8,128)S(1)}, f32[64,128]{1,0:T(8,128)S(1)}, u32[]{:S(2)}, u32[]{:S(2)}) collective-permute-start(f32[64,128]{1,0:T(8,128)S(1)} %get-tuple-element.324), channel_id=1, source_target_pairs={{0,32},{16,48},{32,0},{48,16},{1,33},{17,49},{33,1},{49,17},{2,34}... | collective-permute-start | bytes 98312 | tf_op jit(solution)/shard_map/while/body/eval_jaxpr/ppermute | solution.py:25
  509.9 20.2 %all-to-all-start = ((f32[16,64,128]{2,1,0:T(8,128)}), f32[16,64,128]{2,1,0:T(8,128)S(1)}, u32[]{:S(2)}, u32[]{:S(2)}) async-start(f32[16,64,128]{2,1,0:T(8,128)} %select_reduce_fusion.20), calls=%async_computation | async-start | bytes 1048576 | tf_op jit(solution)/shard_map/while/body/eval_jaxpr/all_to_all | solution.py:59
  513.5 16.6 %collective-permute-start = (f32[64,128]{1,0:T(8,128)S(1)}, f32[64,128]{1,0:T(8,128)S(1)}, u32[]{:S(2)}, u32[]{:S(2)}) collective-permute-start(f32[64,128]{1,0:T(8,128)S(1)} %get-tuple-element.323), channel_id=1, source_target_pairs={{0,48},{16,0},{32,16},{48,32},{1,49},{17,1},{33,17},{49,33},{2,50}... | collective-permute-start | bytes 98312 | tf_op jit(solution)/shard_map/while/body/eval_jaxpr/ppermute | solution.py:25
  513.6 16.5 %collective-permute-start.1 = (f32[64,128]{1,0:T(8,128)S(1)}, f32[64,128]{1,0:T(8,128)S(1)}, u32[]{:S(2)}, u32[]{:S(2)}) collective-permute-start(f32[64,128]{1,0:T(8,128)S(1)} %get-tuple-element.324), channel_id=1, source_target_pairs={{0,32},{16,48},{32,0},{48,16},{1,33},{17,49},{33,1},{49,17},{2,34}... | collective-permute-start | bytes 98312 | tf_op jit(solution)/shard_map/while/body/eval_jaxpr/ppermute | solution.py:25
  (144 other events, 813.1 us)
